TPU v7x, 32 devices: a whole 2x2x4 slice. The times are simulated.
32 devices in a mesh: dom: 4 (over y, x), grp: 8 (over z, core).
Axes of the slice: x: 2, y: 2, z: 4, core: 2. Of those that a mesh axis runs over, the one named last changes fastest.
Arguments:
- features: bfloat16 [40960, 128], P(('dom', 'grp')), may hold values from -6 to 6
- send_dom: int32 [32, 4, 32], P(('dom', 'grp')), may hold values from 0 to 1279
- send_grp: int32 [32, 8, 32], P(('dom', 'grp')), may hold values from 0 to 1279
- tile_vals: bfloat16 [1536, 128, 128], P(('dom', 'grp')), may hold values from 0.049804688 to 1
- tile_tgt: int32 [1536], P(('dom', 'grp')), may hold values from 0 to 9, as said below
- tile_src: int32 [1536], P(('dom', 'grp')), may hold values from 0 to 12, as said below
- tile_count: int32 [32], P(('dom', 'grp')), may hold values from 13 to 48, as said below
- w_self: bfloat16 [128, 256], replicated, may hold values from -0.5 to 0.5
- w_neigh: bfloat16 [128, 256], replicated, may hold values from -0.5 to 0.5
- cotangent: bfloat16 [40960, 256], P(('dom', 'grp'))
Outputs:
- output: bfloat16 [40960, 256], P(('dom', 'grp'))
- grad_features: bfloat16 [40960, 128], P(('dom', 'grp'))
- grad_self: float32 [128, 256], replicated
- grad_neigh: float32 [128, 256], replicated
Inputs may be any that keep to these rules, and one draw needn't show every extreme that they name: `tile_tgt`: in every partition, tile slot t for t < 10 has target block t; other slots name any target block. `tile_src`: in every partition, tile slot t for t < 13 has source block t; other slots name any source block. `tile_count`: some partition has all 48 slots live in every draw.
All inputs are finite; a program needn't handle non-finite values.
Results may differ from a plain program's by a relative error of at most 0.0049.
Values may be sent and summed in bfloat16 or wider, within the bound.
No kernel may reach another device: no remote copies, remote signals or barrier semaphores. Data moves between devices by JAX's collectives and lax.ppermute only.
A program may use at most 64 MiB of HBM per device.

v0:
```python
import jax
import jax.numpy as jnp
from jax import lax
from jax.sharding import PartitionSpec as P


def per_device(
    features,
    send_dom,
    send_grp,
    tile_vals,
    tile_tgt,
    tile_src,
    tile_count,
    w_self,
    w_neigh,
    cotangent,
):
    tile_size = tile_vals.shape[1]
    width = features.shape[1]
    node_count = features.shape[0]
    block_count = node_count // tile_size
    dom_index = send_dom[0]
    grp_index = send_grp[0]
    dom_peers = dom_index.shape[0]
    recv_dom = lax.all_to_all(features[dom_index], "dom", split_axis=0, concat_axis=0, tiled=True)
    recv_grp = lax.all_to_all(features[grp_index], "grp", split_axis=0, concat_axis=0, tiled=True)
    source = jnp.concatenate(
        [features, recv_dom.reshape(-1, width), recv_grp.reshape(-1, width)], axis=0
    )
    source = source.reshape(-1, tile_size, width)
    source_count = source.shape[0]
    slot_count = tile_vals.shape[0]
    usable = jnp.arange(slot_count, dtype=jnp.int32) < tile_count[0]
    to_target = (
        (tile_tgt[None, :] == jnp.arange(block_count, dtype=jnp.int32)[:, None]) & usable[None, :]
    ).astype(jnp.float32)
    to_source = (
        (tile_src[None, :] == jnp.arange(source_count, dtype=jnp.int32)[:, None]) & usable[None, :]
    ).astype(jnp.float32)
    products = jnp.einsum(
        "tij,tjf->tif", tile_vals, source[tile_src], preferred_element_type=jnp.float32
    )
    summed = jnp.einsum("bt,tif->bif", to_target, products, precision=lax.Precision.HIGHEST)
    unit_column = jnp.ones((tile_size,), jnp.bfloat16)
    row_sums = jnp.einsum("tij,j->ti", tile_vals, unit_column, preferred_element_type=jnp.float32)
    degree = jnp.dot(to_target, row_sums, precision=lax.Precision.HIGHEST)
    agg = (summed / degree[:, :, None]).reshape(node_count, width).astype(jnp.bfloat16)
    preact = jnp.dot(features, w_self, preferred_element_type=jnp.float32) + jnp.dot(
        agg, w_neigh, preferred_element_type=jnp.float32
    )
    sigm = jax.nn.sigmoid(preact)
    output = (preact * sigm).astype(jnp.bfloat16)
    grad_pre = (cotangent.astype(jnp.float32) * sigm * (1.0 + preact * (1.0 - sigm))).astype(
        jnp.bfloat16
    )
    part_self = jnp.einsum("nf,nh->fh", features, grad_pre, preferred_element_type=jnp.float32)
    part_neigh = jnp.einsum("nf,nh->fh", agg, grad_pre, preferred_element_type=jnp.float32)
    grad_own = jnp.einsum("nh,fh->nf", grad_pre, w_self, preferred_element_type=jnp.float32)
    grad_agg = jnp.einsum("nh,fh->nf", grad_pre, w_neigh, preferred_element_type=jnp.float32)
    grad_agg = (grad_agg / degree.reshape(-1)[:, None]).astype(jnp.bfloat16)
    picked = grad_agg.reshape(block_count, tile_size, width)[tile_tgt]
    backward = jnp.einsum("tij,tif->tjf", tile_vals, picked, preferred_element_type=jnp.float32)
    grad_source = jnp.einsum(
        "st,tjf->sjf", to_source, backward, precision=lax.Precision.HIGHEST
    ).reshape(-1, width)
    dom_rows = dom_peers * dom_index.shape[1]
    back_dom = (
        grad_source[node_count : node_count + dom_rows]
        .reshape(dom_index.shape[0], dom_index.shape[1], width)
        .astype(jnp.bfloat16)
    )
    back_grp = (
        grad_source[node_count + dom_rows :]
        .reshape(grp_index.shape[0], grp_index.shape[1], width)
        .astype(jnp.bfloat16)
    )
    ret_dom = lax.all_to_all(back_dom, "dom", split_axis=0, concat_axis=0, tiled=True)
    ret_grp = lax.all_to_all(back_grp, "grp", split_axis=0, concat_axis=0, tiled=True)
    grad_self, grad_neigh = lax.psum((part_self, part_neigh), ("dom", "grp"))
    grad_total = grad_own + grad_source[:node_count]
    grad_total = grad_total.at[dom_index.reshape(-1)].add(
        ret_dom.reshape(-1, width).astype(jnp.float32)
    )
    grad_total = grad_total.at[grp_index.reshape(-1)].add(
        ret_grp.reshape(-1, width).astype(jnp.float32)
    )
    return (output, grad_total.astype(jnp.bfloat16), grad_self, grad_neigh)


def solution(mesh):
    return jax.shard_map(
        per_device,
        mesh=mesh,
        in_specs=(
            P(("dom", "grp"), None),
            P(("dom", "grp"), None, None),
            P(("dom", "grp"), None, None),
            P(("dom", "grp"), None, None),
            P(("dom", "grp")),
            P(("dom", "grp")),
            P(("dom", "grp")),
            P(),
            P(),
            P(("dom", "grp"), None),
        ),
        out_specs=(P(("dom", "grp"), None), P(("dom", "grp"), None), P(), P()),
        check_vma=False,
    )
```

profile of v0, /device:TPU:0, one launch (start us, length us, event | category | flops | bytes accessed | tf_op | source)
XLA Modules:
  0.0 210.0 jit_solution(4787525386066854471)
XLA Ops:
  8.1 2.3 %gather_fusion = bf16[128,128]{1,0:T(8,128)(2,1)} fusion(bf16[1280,128]{1,0:T(8,128)(2,1)} %param.10, s32[1024]{0:T(1024)S(1)} %pad_clamp_fusion.3), kind=kCustom, calls=%fused_computation | custom fusion | bytes 66048 | tf_op jit(solution)/shard_map/gather | solution.py:26
  10.4 5.2 %all-to-all-start = ((bf16[4,32,128]{2,1,0:T(8,128)(2,1)}), bf16[4,32,128]{2,1,0:T(8,128)(2,1)S(1)}, u32[]{:S(2)}, u32[]{:S(2)}) async-start(bf16[4,32,128]{2,1,0:T(8,128)(2,1)} %bitcast.3), calls=%async_computation | async-start | bytes 65536 | tf_op jit(solution)/shard_map/all_to_all | solution.py:26
  21.9 1.5 gather_fusion.1
  23.4 4.9 %all-to-all-start.1 = ((bf16[8,32,128]{2,1,0:T(8,128)(2,1)}), bf16[8,32,128]{2,1,0:T(8,128)(2,1)S(1)}, u32[]{:S(2)}, u32[]{:S(2)}) async-start(bf16[8,32,128]{2,1,0:T(8,128)(2,1)} %bitcast.6), calls=%async_computation.1 | async-start | bytes 131072 | tf_op jit(solution)/shard_map/all_to_all | solution.py:27
  28.4 5.8 %all-to-all-done.1 = bf16[8,32,128]{2,1,0:T(8,128)(2,1)S(1)} async-done(((bf16[8,32,128]{2,1,0:T(8,128)(2,1)}), bf16[8,32,128]{2,1,0:T(8,128)(2,1)S(1)}, u32[]{:S(2)}, u32[]{:S(2)}) %all-to-all-start.1) | async-done | bytes 65568 | tf_op jit(solution)/shard_map/all_to_all | solution.py:27
  34.2 1.9 gather_fusion.2
  36.1 4.3 %fusion.35 = f32[48,128,128]{2,1,0:T(8,128)} fusion(bf16[48,128,128]{2,1,0:T(8,128)(2,1)} %gather_fusion.2, bf16[48,128,128]{2,1,0:T(8,128)(2,1)S(1)} %copy-done), kind=kOutput, calls=%fused_computation.55 | convolution fusion | flops 201326592 | bytes 6291456 | tf_op jit(solution)/shard_map/tij,tjf->tif/dot_general | solution.py:41
  40.4 3.6 %copy.22 = f32[48,128,128]{1,0,2:T(8,128)} copy(f32[48,128,128]{2,1,0:T(8,128)} %fusion.35) | data formatting | bytes 6291456 | tf_op jit(solution)/shard_map/tij,tjf->tif/dot_general | solution.py:41
  44.1 3.3 %fusion.8 = bf16[10,128,128]{2,0,1:T(8,128)(2,1)S(1)} fusion(f32[48,128,128]{1,0,2:T(8,128)} %copy.22, f32[10,128]{0,1:T(8,128)S(1)} %copy.17, s32[48]{0:T(128)S(1)} %copy-done.5, pred[48]{0:T(512)(128)(4,1)S(1)} %iota_compare_fusion.2), kind=kOutput, calls=%fused_computation.18 | convolution fusion | flops 94700480 | bytes 3478768 | tf_op jit(solution)/shard_map/bt,tif->bif/dot_general | solution.py:44
  47.5 1.6 multiply_convert_fusion
  50.4 1.9 gather_fusion.3
  52.3 3.7 %fusion.36 = f32[48,128,128]{2,1,0:T(8,128)} fusion(bf16[48,128,128]{2,1,0:T(8,128)(2,1)} %gather_fusion.3, bf16[48,128,128]{2,1,0:T(8,128)(2,1)S(1)} %copy-done), kind=kOutput, calls=%fused_computation.56 | convolution fusion | flops 201326592 | bytes 6291456 | tf_op jit(solution)/shard_map/tij,tif->tjf/dot_general | solution.py:63
  56.1 3.6 %copy.24 = f32[48,128,128]{1,0,2:T(8,128)} copy(f32[48,128,128]{2,1,0:T(8,128)} %fusion.36) | data formatting | bytes 6291456 | tf_op jit(solution)/shard_map/tij,tif->tjf/dot_general | solution.py:63
  59.7 4.0 %fusion.33 = (bf16[13,128,128]{2,0,1:T(8,128)(2,1)S(1)}, f32[13,128,128]{2,0,1:T(8,128)}) fusion(f32[48,128,128]{1,0,2:T(8,128)} %copy.24, s32[48]{0:T(128)S(1)} %copy-done.6, pred[48]{0:T(512)(128)(4,1)S(1)} %iota_compare_fusion.2), kind=kOutput, calls=%fused_computation.53 | convolution fusion | flops 122897632 | bytes 4423920 | tf_op jit(solution)/shard_map/st,tjf->sjf/dot_general | solution.py:64
  64.4 4.2 %all-to-all-start.2 = ((bf16[4,32,128]{2,1,0:T(8,128)(2,1)}), bf16[4,32,128]{2,1,0:T(8,128)(2,1)S(1)}, u32[]{:S(2)}, u32[]{:S(2)}) async-start(bf16[4,32,128]{2,1,0:T(8,128)(2,1)} %bitcast.26), calls=%async_computation.2 | async-start | bytes 65536 | tf_op jit(solution)/shard_map/all_to_all | solution.py:78
  71.8 1.5 all-to-all-done.2
  73.4 3.4 %all-to-all-start.3 = ((bf16[8,32,128]{2,1,0:T(8,128)(2,1)}), bf16[8,32,128]{2,1,0:T(8,128)(2,1)S(1)}, u32[]{:S(2)}, u32[]{:S(2)}) async-start(bf16[8,32,128]{2,1,0:T(8,128)(2,1)} %bitcast.21), calls=%async_computation.3 | async-start | bytes 131072 | tf_op jit(solution)/shard_map/all_to_all | solution.py:79
  77.9 3.1 %scatter_custom_fusion = f32[1280,128]{1,0:T(8,128)} fusion(f32[1280,128]{1,0:T(8,128)} %convolution_add_fusion.1, s32[128]{0:T(128)S(1)} %fusion.29, bf16[128,128]{1,0:T(8,128)(2,1)S(1)} %bitcast.80), kind=kCustom, calls=%fused_computation.23 | custom fusion | flops 32768 | bytes 688128 | tf_op jit(solution)/shard_map/scatter-add | solution.py:82
  81.0 1.6 all-to-all-done.3
  82.6 3.7 %scatter_custom_fusion.1 = f32[1280,128]{1,0:T(8,128)} fusion(f32[1280,128]{1,0:T(8,128)} %scatter_custom_fusion, s32[256]{0:T(256)S(1)} %bitcast.83, bf16[256,128]{1,0:T(8,128)(2,1)S(1)} %bitcast.77), kind=kCustom, calls=%fused_computation.21 | custom fusion | flops 65536 | bytes 720896 | tf_op jit(solution)/shard_map/scatter-add | solution.py:85
  86.3 1.8 convert_element_type.55
  88.1 111.7 %all-reduce.3.cloned.1.call-done = (f32[128,256]{0,1:T(8,128)}, f32[128,256]{1,0:T(8,128)}) async-done(((f32[128,256]{0,1:T(8,128)}, f32[128,256]{1,0:T(8,128)}), (f32[128,256]{0,1:T(8,128)}, f32[128,256]{1,0:T(8,128)})) %all-reduce.3.cloned.1.call-update) | async-done | bytes 262160 | tf_op jit(solution)/shard_map/psum | solution.py:80
  199.9 1.7 copy.21
  201.5 1.6 copy.31
  (51 shorter events, 13.2 us)
Async XLA Ops:
  7.2 12.7 %copy-start = (bf16[48,128,128]{2,1,0:T(8,128)(2,1)S(1)}, bf16[48,128,128]{2,1,0:T(8,128)(2,1)}, u32[]{:S(2)}) copy-start(bf16[48,128,128]{2,1,0:T(8,128)(2,1)} %param.13) | copy-start | bytes 4718596
  7.2 13.2 %copy-start.1 = (bf16[1280,128]{1,0:T(8,128)(2,1)S(1)}, bf16[1280,128]{1,0:T(8,128)(2,1)}, u32[]{:S(2)}) copy-start(bf16[1280,128]{1,0:T(8,128)(2,1)} %param.10) | copy-start | bytes 983044
  7.2 13.2 %copy-start.3 = (bf16[128,256]{1,0:T(8,128)(2,1)S(1)}, bf16[128,256]{1,0:T(8,128)(2,1)}, u32[]{:S(2)}) copy-start(bf16[128,256]{1,0:T(8,128)(2,1)} %param.17) | copy-start | bytes 196612
  10.4 13.0 %all-to-all-start = ((bf16[4,32,128]{2,1,0:T(8,128)(2,1)}), bf16[4,32,128]{2,1,0:T(8,128)(2,1)S(1)}, u32[]{:S(2)}, u32[]{:S(2)}) async-start(bf16[4,32,128]{2,1,0:T(8,128)(2,1)} %bitcast.3), calls=%async_computation | async-start | bytes 65536 | tf_op jit(solution)/shard_map/all_to_all | solution.py:26
  19.8 1.9 copy-start.5
  23.4 10.8 %all-to-all-start.1 = ((bf16[8,32,128]{2,1,0:T(8,128)(2,1)}), bf16[8,32,128]{2,1,0:T(8,128)(2,1)S(1)}, u32[]{:S(2)}, u32[]{:S(2)}) async-start(bf16[8,32,128]{2,1,0:T(8,128)(2,1)} %bitcast.6), calls=%async_computation.1 | async-start | bytes 131072 | tf_op jit(solution)/shard_map/all_to_all | solution.py:27
  44.1 3.4 %copy-start.2 = (f32[1280,256]{1,0:T(8,128)S(1)}, f32[1280,256]{1,0:T(8,128)}, u32[]{:S(2)}) copy-start(f32[1280,256]{1,0:T(8,128)} %fusion.34) | copy-start | bytes 3932164
  44.1 3.4 %copy-start.7 = (bf16[1280,256]{1,0:T(8,128)(2,1)S(1)}, bf16[1280,256]{1,0:T(8,128)(2,1)}, u32[]{:S(2)}) copy-start(bf16[1280,256]{1,0:T(8,128)(2,1)} %param.19) | copy-start | bytes 1966084
  44.1 3.4 %copy-start.8 = (bf16[128,256]{1,0:T(8,128)(2,1)S(1)}, bf16[128,256]{1,0:T(8,128)(2,1)}, u32[]{:S(2)}) copy-start(bf16[128,256]{1,0:T(8,128)(2,1)} %param.18) | copy-start | bytes 196612
  56.1 3.6 %copy-start.6 = (s32[48]{0:T(128)S(1)}, s32[48]{0:T(128)}, u32[]{:S(2)}) copy-start(s32[48]{0:T(128)} %param.15) | copy-start | bytes 580
  64.4 9.0 %all-to-all-start.2 = ((bf16[4,32,128]{2,1,0:T(8,128)(2,1)}), bf16[4,32,128]{2,1,0:T(8,128)(2,1)S(1)}, u32[]{:S(2)}, u32[]{:S(2)}) async-start(bf16[4,32,128]{2,1,0:T(8,128)(2,1)} %bitcast.26), calls=%async_computation.2 | async-start | bytes 65536 | tf_op jit(solution)/shard_map/all_to_all | solution.py:78
  68.6 8.1 %copy-start.4 = (bf16[128,256]{1,0:T(8,128)(2,1)S(1)}, bf16[128,256]{1,0:T(8,128)(2,1)}, u32[]{:S(2)}) copy-start(bf16[128,256]{1,0:T(8,128)(2,1)} %param.17) | copy-start | bytes 196612
  68.6 131.3 %all-reduce.3.cloned.1.call-start = ((), (), s32[]{:S(2)}) async-start(), calls=%async_computation.4 | async-start | bytes 524288 | tf_op jit(solution)/shard_map/psum | solution.py:80
  73.4 9.2 %all-to-all-start.3 = ((bf16[8,32,128]{2,1,0:T(8,128)(2,1)}), bf16[8,32,128]{2,1,0:T(8,128)(2,1)S(1)}, u32[]{:S(2)}, u32[]{:S(2)}) async-start(bf16[8,32,128]{2,1,0:T(8,128)(2,1)} %bitcast.21), calls=%async_computation.3 | async-start | bytes 131072 | tf_op jit(solution)/shard_map/all_to_all | solution.py:79
Sparse Core Ops, SparseCore 0:
  75.7 124.1 all-reduce.2
where the time goes:
time: 211 us; the launch traced here: 210 us
  waiting for transfers between devices  121 us (57%)
  local copies, waits for them, and re-layouts  22.9 us (11%)
  matrix products  22.5 us (11%)
  starting transfers between devices  17.6 us (8%)
  between operations  14.8 us (7%)
  other arithmetic  11.5 us (5%)
    psum x1, waiting for transfers between devices, per_device(): grad_self, grad_neigh = lax.psum((part_self, part_neigh), ('dom', 'grp'))  112 us
    all_to_all x1, waiting for transfers between devices, per_device(): lax.all_to_all(features[grp_index], 'grp', split_axis=0, concat_axis=0, t...  5.79 us
    all_to_all x1, starting transfers between devices, per_device(): lax.all_to_all(features[dom_index], 'dom', split_axis=0, concat_axis=0, t...  5.16 us
    all_to_all x1, starting transfers between devices, per_device(): lax.all_to_all(features[grp_index], 'grp', split_axis=0, concat_axis=0, t...  4.88 us
    dot_general x1, matrix products, per_device(): jnp.einsum('tij,tjf->tif', tile_vals, source[tile_src], preferred_element...  4.3 us
  transfers between devices with their start and end apart: 5, of which 4 were waited for; matrix products, arithmetic and copies ran while one was open for 10% of the time, Pallas kernels for 0%

commit v1 on v0

--- a/solution.py
+++ b/solution.py
@@ -2,6 +2,27 @@
 import jax.numpy as jnp
 from jax import lax
 from jax.sharding import PartitionSpec as P
+
+
+def make_the_stacks_all(array_in):
+    outcome_arr = jax.lax.axis_index("dom")
+    new = jax.lax.axis_size("dom")
+    block_last, n_now = (new, outcome_arr)
+    frame_out = array_in.shape[0] // block_last
+    tall = list(array_in.shape)
+    tall[0] = frame_out
+    low = tall[0]
+    tall[0] = low * block_last
+    met_up = jnp.zeros(tall, array_in.dtype)
+    for at in tuple(range(block_last)):
+        z = lax.dynamic_slice_in_dim(array_in, (n_now ^ at) * frame_out, frame_out, axis=0)
+        if at:
+            sides = []
+            for it in tuple(range(block_last)):
+                sides.append((it, it ^ at))
+            z = jax.lax.ppermute(z, "dom", sides)
+        met_up = lax.dynamic_update_slice_in_dim(met_up, z, (n_now ^ at) * low, axis=0)
+    return met_up
 
 
 def per_device(
@@ -23,7 +44,7 @@
     dom_index = send_dom[0]
     grp_index = send_grp[0]
     dom_peers = dom_index.shape[0]
-    recv_dom = lax.all_to_all(features[dom_index], "dom", split_axis=0, concat_axis=0, tiled=True)
+    recv_dom = make_the_stacks_all(features[dom_index])
     recv_grp = lax.all_to_all(features[grp_index], "grp", split_axis=0, concat_axis=0, tiled=True)
     source = jnp.concatenate(
         [features, recv_dom.reshape(-1, width), recv_grp.reshape(-1, width)], axis=0

time: 211 us -> 207 us (0.981)
  other arithmetic: 11.5 us -> 7.23 us
    all_to_all x1 -> x0, starting transfers between devices: 5.16 us -> none  [per_device(): lax.all_to_all(features[dom_index], 'dom', split_axis=0, concat_axis=0, t...]
    all_to_all x1, waiting for transfers between devices: 5.79 us -> 0.78 us  [per_device(): lax.all_to_all(features[grp_index], 'grp', split_axis=0, concat_axis=0, t...]
    ppermute x0 -> x3, starting transfers between devices: none -> 4.54 us  [make_the_stacks_all(): z = jax.lax.ppermute(z, 'dom', sides)]
    psum x1, waiting for transfers between devices: 112 us -> 115 us  [per_device(): grad_self, grad_neigh = lax.psum((part_self, part_neigh), ('dom', 'grp'))]
  transfers between devices with their start and end apart: 5 -> 7, of which waited for: 4 -> 4; matrix products, arithmetic and copies ran while one was open for 10% -> 8% of each run, Pallas kernels for 0% -> 0%
where the time goes in v1:
time: 207 us; the launch traced here: 206 us
  waiting for transfers between devices  121 us (58%)
  local copies, waits for them, and re-layouts  23.2 us (11%)
  matrix products  22.5 us (11%)
  starting transfers between devices  17.9 us (9%)
  between operations  14.9 us (7%)
  other arithmetic  7.23 us (3%)
    psum x1, waiting for transfers between devices, per_device(): grad_self, grad_neigh = lax.psum((part_self, part_neigh), ('dom', 'grp'))  115 us
    all_to_all x1, starting transfers between devices, per_device(): lax.all_to_all(features[grp_index], 'grp', split_axis=0, concat_axis=0, t...  5.33 us
    ppermute x3, starting transfers between devices, make_the_stacks_all(): z = jax.lax.ppermute(z, 'dom', sides)  4.54 us
    all_to_all x1, starting transfers between devices, per_device(): lax.all_to_all(back_grp, 'grp', split_axis=0, concat_axis=0, tiled=True)  4.33 us
    dot_general x1, matrix products, per_device(): jnp.einsum('tij,tjf->tif', tile_vals, source[tile_src], preferred_element...  4.3 us
  transfers between devices with their start and end apart: 7, of which 4 were waited for; matrix products, arithmetic and copies ran while one was open for 8% of the time, Pallas kernels for 0%

profile of v1, /device:TPU:0, one launch (start us, length us, event | category | flops | bytes accessed | tf_op | source)
XLA Modules:
  0.0 206.3 jit_solution(2229529775570928119)
XLA Ops:
  8.1 1.7 gather_fusion
  9.8 3.0 %collective-permute-start = (bf16[1,32,128]{2,1,0:T(8,128)(2,1)S(1)}, bf16[1,32,128]{2,1,0:T(8,128)(2,1)S(1)}, u32[]{:S(2)}, u32[]{:S(2)}) collective-permute-start(bf16[1,32,128]{2,1,0:T(8,128)(2,1)S(1)} %get-tuple-element.18), channel_id=1, source_target_pairs={{0,8},{8,0},{16,24},{24,16},{1,9},{9,1},{17,25},{25,17},{2,10},{10... | collective-permute-start | bytes 24584 | tf_op jit(solution)/shard_map/ppermute | solution.py:23
  12.8 1.5 collective-permute-start.1
  15.2 2.4 %gather_fusion.1 = bf16[256,128]{1,0:T(8,128)(2,1)} fusion(bf16[1280,128]{1,0:T(8,128)(2,1)} %param.10, s32[1024]{0:T(1024)S(1)} %pad_clamp_fusion.2), kind=kCustom, calls=%fused_computation.1 | custom fusion | bytes 132096 | tf_op jit(solution)/shard_map/gather | solution.py:48
  17.5 5.3 %all-to-all-start = ((bf16[8,32,128]{2,1,0:T(8,128)(2,1)}), bf16[8,32,128]{2,1,0:T(8,128)(2,1)S(1)}, u32[]{:S(2)}, u32[]{:S(2)}) async-start(bf16[8,32,128]{2,1,0:T(8,128)(2,1)} %bitcast.6), calls=%async_computation | async-start | bytes 131072 | tf_op jit(solution)/shard_map/all_to_all | solution.py:48
  28.8 2.0 gather_fusion.2
  30.8 4.3 %fusion.35 = f32[48,128,128]{2,1,0:T(8,128)} fusion(bf16[48,128,128]{2,1,0:T(8,128)(2,1)} %gather_fusion.2, bf16[48,128,128]{2,1,0:T(8,128)(2,1)S(1)} %copy-done), kind=kOutput, calls=%fused_computation.62 | convolution fusion | flops 201326592 | bytes 6291456 | tf_op jit(solution)/shard_map/tij,tjf->tif/dot_general | solution.py:62
  35.1 3.6 %copy.22 = f32[48,128,128]{1,0,2:T(8,128)} copy(f32[48,128,128]{2,1,0:T(8,128)} %fusion.35) | data formatting | bytes 6291456 | tf_op jit(solution)/shard_map/tij,tjf->tif/dot_general | solution.py:62
  38.7 3.3 %fusion.8 = bf16[10,128,128]{2,0,1:T(8,128)(2,1)S(1)} fusion(f32[48,128,128]{1,0,2:T(8,128)} %copy.22, f32[10,128]{0,1:T(8,128)S(1)} %copy.17, s32[48]{0:T(128)S(1)} %copy-done.5, pred[48]{0:T(512)(128)(4,1)S(1)} %iota_compare_fusion.2), kind=kOutput, calls=%fused_computation.18 | convolution fusion | flops 94700480 | bytes 3478768 | tf_op jit(solution)/shard_map/bt,tif->bif/dot_general | solution.py:65
  42.1 1.7 multiply_convert_fusion
  45.0 2.0 gather_fusion.3
  47.0 3.7 %fusion.36 = f32[48,128,128]{2,1,0:T(8,128)} fusion(bf16[48,128,128]{2,1,0:T(8,128)(2,1)} %gather_fusion.3, bf16[48,128,128]{2,1,0:T(8,128)(2,1)S(1)} %copy-done), kind=kOutput, calls=%fused_computation.63 | convolution fusion | flops 201326592 | bytes 6291456 | tf_op jit(solution)/shard_map/tij,tif->tjf/dot_general | solution.py:84
  50.7 3.6 %copy.24 = f32[48,128,128]{1,0,2:T(8,128)} copy(f32[48,128,128]{2,1,0:T(8,128)} %fusion.36) | data formatting | bytes 6291456 | tf_op jit(solution)/shard_map/tij,tif->tjf/dot_general | solution.py:84
  54.3 4.0 %fusion.33 = (bf16[13,128,128]{2,0,1:T(8,128)(2,1)S(1)}, f32[13,128,128]{2,0,1:T(8,128)}) fusion(f32[48,128,128]{1,0,2:T(8,128)} %copy.24, s32[48]{0:T(128)S(1)} %copy-done.6, pred[48]{0:T(512)(128)(4,1)S(1)} %iota_compare_fusion.2), kind=kOutput, calls=%fused_computation.60 | convolution fusion | flops 122897632 | bytes 4423920 | tf_op jit(solution)/shard_map/st,tjf->sjf/dot_general | solution.py:85
  59.1 3.7 %all-to-all-start.1 = ((bf16[4,32,128]{2,1,0:T(8,128)(2,1)}), bf16[4,32,128]{2,1,0:T(8,128)(2,1)S(1)}, u32[]{:S(2)}, u32[]{:S(2)}) async-start(bf16[4,32,128]{2,1,0:T(8,128)(2,1)} %bitcast.26), calls=%async_computation.1 | async-start | bytes 65536 | tf_op jit(solution)/shard_map/all_to_all | solution.py:99
  63.9 1.4 copy.19
  66.0 1.5 all-to-all-done.1
  67.5 4.3 %all-to-all-start.2 = ((bf16[8,32,128]{2,1,0:T(8,128)(2,1)}), bf16[8,32,128]{2,1,0:T(8,128)(2,1)}, u32[]{:S(2)}, u32[]{:S(2)}) async-start(bf16[8,32,128]{2,1,0:T(8,128)(2,1)} %bitcast.21), calls=%async_computation.2 | async-start | bytes 131072 | tf_op jit(solution)/shard_map/all_to_all | solution.py:100
  73.0 1.7 scatter_custom_fusion
  74.8 3.1 %all-to-all-done.2 = bf16[8,32,128]{2,1,0:T(8,128)(2,1)} async-done(((bf16[8,32,128]{2,1,0:T(8,128)(2,1)}), bf16[8,32,128]{2,1,0:T(8,128)(2,1)}, u32[]{:S(2)}, u32[]{:S(2)}) %all-to-all-start.2) | async-done | bytes 65568 | tf_op jit(solution)/shard_map/all_to_all | solution.py:100
  77.9 2.5 %scatter_custom_fusion.1 = f32[1280,128]{1,0:T(8,128)S(1)} fusion(f32[1280,128]{1,0:T(8,128)S(1)} %scatter_custom_fusion, s32[256]{0:T(256)S(1)} %bitcast.83, bf16[256,128]{1,0:T(8,128)(2,1)} %bitcast.25), kind=kCustom, calls=%fused_computation.21 | custom fusion | flops 65536 | bytes 720896 | tf_op jit(solution)/shard_map/scatter-add | solution.py:106
  81.1 115.1 %all-reduce.3.cloned.1.call-done = (f32[128,256]{0,1:T(8,128)}, f32[128,256]{1,0:T(8,128)}) async-done(((f32[128,256]{0,1:T(8,128)}, f32[128,256]{1,0:T(8,128)}), (f32[128,256]{0,1:T(8,128)}, f32[128,256]{1,0:T(8,128)})) %all-reduce.3.cloned.1.call-update) | async-done | bytes 262160 | tf_op jit(solution)/shard_map/psum | solution.py:101
  196.2 1.7 copy.21
  197.9 1.6 copy.35
  (60 shorter events, 12.7 us)
Async XLA Ops:
  7.2 18.6 %copy-start = (bf16[48,128,128]{2,1,0:T(8,128)(2,1)S(1)}, bf16[48,128,128]{2,1,0:T(8,128)(2,1)}, u32[]{:S(2)}) copy-start(bf16[48,128,128]{2,1,0:T(8,128)(2,1)} %param.13) | copy-start | bytes 4718596
  7.2 19.1 %copy-start.1 = (bf16[1280,128]{1,0:T(8,128)(2,1)S(1)}, bf16[1280,128]{1,0:T(8,128)(2,1)}, u32[]{:S(2)}) copy-start(bf16[1280,128]{1,0:T(8,128)(2,1)} %param.10) | copy-start | bytes 983044
  7.2 19.1 %copy-start.3 = (bf16[128,256]{1,0:T(8,128)(2,1)S(1)}, bf16[128,256]{1,0:T(8,128)(2,1)}, u32[]{:S(2)}) copy-start(bf16[128,256]{1,0:T(8,128)(2,1)} %param.17) | copy-start | bytes 196612
  9.8 18.1 %collective-permute-start = (bf16[1,32,128]{2,1,0:T(8,128)(2,1)S(1)}, bf16[1,32,128]{2,1,0:T(8,128)(2,1)S(1)}, u32[]{:S(2)}, u32[]{:S(2)}) collective-permute-start(bf16[1,32,128]{2,1,0:T(8,128)(2,1)S(1)} %get-tuple-element.18), channel_id=1, source_target_pairs={{0,8},{8,0},{16,24},{24,16},{1,9},{9,1},{17,25},{25,17},{2,10},{10... | collective-permute-start | bytes 24584 | tf_op jit(solution)/shard_map/ppermute | solution.py:23
  12.8 15.1 %collective-permute-start.1 = (bf16[1,32,128]{2,1,0:T(8,128)(2,1)S(1)}, bf16[1,32,128]{2,1,0:T(8,128)(2,1)S(1)}, u32[]{:S(2)}, u32[]{:S(2)}) collective-permute-start(bf16[1,32,128]{2,1,0:T(8,128)(2,1)S(1)} %get-tuple-element.17), channel_id=1, source_target_pairs={{0,16},{8,24},{16,0},{24,8},{1,17},{9,25},{17,1},{25,9},{2,18},{10... | collective-permute-start | bytes 24584 | tf_op jit(solution)/shard_map/ppermute | solution.py:23
  14.4 13.6 %collective-permute-start.2 = (bf16[1,32,128]{2,1,0:T(8,128)(2,1)S(1)}, bf16[1,32,128]{2,1,0:T(8,128)(2,1)S(1)}, u32[]{:S(2)}, u32[]{:S(2)}) collective-permute-start(bf16[1,32,128]{2,1,0:T(8,128)(2,1)S(1)} %get-tuple-element.16), channel_id=1, source_target_pairs={{0,24},{8,16},{16,8},{24,0},{1,25},{9,17},{17,9},{25,1},{2,26},{10... | collective-permute-start | bytes 24584 | tf_op jit(solution)/shard_map/ppermute | solution.py:23
  17.5 11.2 %all-to-all-start = ((bf16[8,32,128]{2,1,0:T(8,128)(2,1)}), bf16[8,32,128]{2,1,0:T(8,128)(2,1)S(1)}, u32[]{:S(2)}, u32[]{:S(2)}) async-start(bf16[8,32,128]{2,1,0:T(8,128)(2,1)} %bitcast.6), calls=%async_computation | async-start | bytes 131072 | tf_op jit(solution)/shard_map/all_to_all | solution.py:48
  25.7 1.9 copy-start.5
  38.7 3.4 %copy-start.2 = (f32[1280,256]{1,0:T(8,128)S(1)}, f32[1280,256]{1,0:T(8,128)}, u32[]{:S(2)}) copy-start(f32[1280,256]{1,0:T(8,128)} %fusion.34) | copy-start | bytes 3932164
  38.7 3.4 %copy-start.7 = (bf16[1280,256]{1,0:T(8,128)(2,1)S(1)}, bf16[1280,256]{1,0:T(8,128)(2,1)}, u32[]{:S(2)}) copy-start(bf16[1280,256]{1,0:T(8,128)(2,1)} %param.19) | copy-start | bytes 1966084
  38.7 3.4 %copy-start.8 = (bf16[128,256]{1,0:T(8,128)(2,1)S(1)}, bf16[128,256]{1,0:T(8,128)(2,1)}, u32[]{:S(2)}) copy-start(bf16[128,256]{1,0:T(8,128)(2,1)} %param.18) | copy-start | bytes 196612
  50.7 3.6 %copy-start.6 = (s32[48]{0:T(128)S(1)}, s32[48]{0:T(128)}, u32[]{:S(2)}) copy-start(s32[48]{0:T(128)} %param.15) | copy-start | bytes 580
  59.1 8.5 %all-to-all-start.1 = ((bf16[4,32,128]{2,1,0:T(8,128)(2,1)}), bf16[4,32,128]{2,1,0:T(8,128)(2,1)S(1)}, u32[]{:S(2)}, u32[]{:S(2)}) async-start(bf16[4,32,128]{2,1,0:T(8,128)(2,1)} %bitcast.26), calls=%async_computation.1 | async-start | bytes 65536 | tf_op jit(solution)/shard_map/all_to_all | solution.py:99
  62.8 133.5 %all-reduce.3.cloned.1.call-start = ((), (), s32[]{:S(2)}) async-start(), calls=%async_computation.3 | async-start | bytes 524288 | tf_op jit(solution)/shard_map/psum | solution.py:101
  67.5 4.3 %copy-start.4 = (bf16[4,32,128]{2,1,0:T(8,128)(2,1)}, bf16[4,32,128]{2,1,0:T(8,128)(2,1)S(1)}, u32[]{:S(2)}) copy-start(bf16[4,32,128]{2,1,0:T(8,128)(2,1)S(1)} %all-to-all-done.1) | copy-start | bytes 98308
  67.5 10.4 %all-to-all-start.2 = ((bf16[8,32,128]{2,1,0:T(8,128)(2,1)}), bf16[8,32,128]{2,1,0:T(8,128)(2,1)}, u32[]{:S(2)}, u32[]{:S(2)}) async-start(bf16[8,32,128]{2,1,0:T(8,128)(2,1)} %bitcast.21), calls=%async_computation.2 | async-start | bytes 131072 | tf_op jit(solution)/shard_map/all_to_all | solution.py:100
Sparse Core Ops, SparseCore 0:
  69.8 126.3 all-reduce.2
